TPU v7x, 512 devices: a whole 4x8x8 slice. The times are simulated.
512 devices in a mesh: section: 32 (over z, x), et: 16 (over y, core).
Axes of the slice: x: 4, y: 8, z: 8, core: 2. Of those that a mesh axis runs over, the one named last changes fastest.
Arguments:
- x_fwd: bfloat16 [32, 256, 3072], P('section', 'et'), may hold values from -6 to 6
- act_fwd: bfloat16 [32, 256, 8192], P('section', None, 'et'), may hold values from -6 to 6
- ids_fwd: int32 [32, 256, 2], P('section'), may hold values from 0 to 7, as said below
- x_bwd: bfloat16 [32, 256, 3072], P('section', 'et'), may hold values from -6 to 6
- act_bwd: bfloat16 [32, 256, 8192], P('section', None, 'et'), may hold values from -6 to 6
- ids_bwd: int32 [32, 256, 2], P('section'), may hold values from 0 to 7, as said below
- grad_out: bfloat16 [32, 256, 3072], P('section', 'et'), may hold values from -6 to 6
- gain: bfloat16 [32, 3072], P('section'), may hold values from 0.099609375 to 1.8984375
- w_router: bfloat16 [32, 3072, 8], P('section'), may hold values from -0.21875 to 0.21875
- w_down: bfloat16 [32, 8192, 3072], P('section', 'et'), may hold values from -0.0625 to 0.0625
Outputs:
- fwd_in: bfloat16 [32, 256, 3072], P('section', 'et')
- incoming_gradient: bfloat16 [32, 256, 3072], P('section', 'et')
- dact: bfloat16 [32, 256, 8192], P('section', None, 'et')
Inputs may be any that keep to these rules, and one draw needn't show every extreme that they name: `ids_fwd`: each token names 2 different experts; in each section's micro-batch exactly 128 tokens name expert 0. `ids_bwd`: each token names 2 different experts; in each section's micro-batch exactly 128 tokens name expert 0.
All inputs are finite; a program needn't handle non-finite values.
Results may differ from a plain program's by a relative error of at most 0.014.
Values may be sent and summed in bfloat16 or wider, within the bound.
No kernel may reach another device: no remote copies, remote signals or barrier semaphores. Data moves between devices by JAX's collectives and lax.ppermute only.
A program may use at most 64 MiB of HBM per device.

v0:
```python
import jax
import jax.numpy as jnp
from jax import lax
from jax.sharding import PartitionSpec as P


def from_behind(value, axis, steps):
    count = lax.axis_size(axis)
    first, last = (max(0, -steps), min(count, count - steps))
    return lax.ppermute(value, axis, [(source, source + steps) for source in range(first, last)])


def norm_logits(inputs, gain, w_router):
    wide = inputs.astype(jnp.float32)
    inverse = lax.rsqrt(jnp.mean(wide * wide, axis=-1, keepdims=True) + 1e-05)
    normed = (wide * inverse * gain.astype(jnp.float32)).astype(jnp.bfloat16)
    logits = jnp.dot(normed, w_router, preferred_element_type=jnp.float32).astype(jnp.bfloat16)
    return (wide, inverse, logits)


def routing(logits, chosen, experts):
    route = jnp.sum((chosen == 0).astype(jnp.float32), axis=1)
    partner = jnp.minimum(jnp.sum(chosen, axis=1), experts - 1)
    labels = jnp.arange(experts, dtype=jnp.int32)
    onehot = (partner[:, None] == labels[None, :]).astype(jnp.float32)
    wide_logits = logits.astype(jnp.float32)
    sigma = jax.nn.sigmoid(wide_logits[:, 0] - jnp.sum(wide_logits * onehot, axis=1))
    return (route, onehot, sigma, route * sigma)


def arrange(chosen):
    member = jnp.sum((chosen == 0).astype(jnp.int32), axis=1)
    tally = jnp.sum(member)
    before = jnp.cumsum(member) - member
    after = jnp.cumsum(1 - member) - (1 - member)
    place = jnp.where(member == 1, before, tally + after)
    ordering = jnp.zeros_like(member).at[place].set(jnp.arange(member.shape[0], dtype=jnp.int32))
    return (member, place, ordering)


def spread_back(compact, member, place, capacity):
    safe = jnp.minimum(place, capacity - 1)
    return jnp.where(member[:, None] == 1, compact[safe], 0.0)


def shards(x_fwd, act_fwd, ids_fwd, x_bwd, act_bwd, ids_bwd, grad_out, gain, w_router, w_down):
    x_fwd, act_fwd, ids_fwd, x_bwd, act_bwd = (
        x_fwd[0],
        act_fwd[0],
        ids_fwd[0],
        x_bwd[0],
        act_bwd[0],
    )
    ids_bwd, grad_out, gain, w_router, w_down = (
        ids_bwd[0],
        grad_out[0],
        gain[0],
        w_router[0],
        w_down[0],
    )
    experts = w_router.shape[1]
    tokens = ids_fwd.shape[0]
    capacity = tokens // 2
    own_rows = x_fwd.shape[0]
    first_row = lax.axis_index("et") * own_rows
    wide_f, inverse_f, logit_f = norm_logits(x_fwd, gain, w_router)
    backward_wide_rows, backward_inverse_norm, logit_b = norm_logits(x_bwd, gain, w_router)
    full_f, full_b, full_g = (
        lax.all_gather(logit_f, "et", axis=0, tiled=True),
        lax.all_gather(logit_b, "et", axis=0, tiled=True),
        lax.all_gather(grad_out, "et", axis=0, tiled=True),
    )
    route_f, onehot_f, sigma_f, coef_f = routing(full_f, ids_fwd, experts)
    member_f, place_f, order_f = arrange(ids_fwd)
    chosen_f = order_f[:capacity]
    compact = (
        jnp.dot(act_fwd[chosen_f], w_down, preferred_element_type=jnp.float32)
        * coef_f[chosen_f][:, None]
    )
    summed = lax.psum(compact.astype(jnp.bfloat16), "et").astype(jnp.float32)
    member_own = lax.dynamic_slice_in_dim(member_f, first_row, own_rows, 0)
    place_own = lax.dynamic_slice_in_dim(place_f, first_row, own_rows, 0)
    y_mine = spread_back(summed, member_own, place_own, capacity)
    layer_out = (wide_f + y_mine).astype(jnp.bfloat16)
    route_b, onehot_b, sigma_b, backward_coefficient = routing(full_b, ids_bwd, experts)
    member_b, place_b, order_b = arrange(ids_bwd)
    chosen_b = order_b[:capacity]
    up_compact = lax.dot_general(
        full_g[chosen_b], w_down, (((1,), (1,)), ((), ())), preferred_element_type=jnp.float32
    )
    back_up = spread_back(up_compact, member_b, place_b, capacity)
    dact = (backward_coefficient[:, None] * back_up).astype(jnp.bfloat16)
    dprob_part = jnp.sum(act_bwd.astype(jnp.float32) * back_up, axis=1)
    dprob_all = lax.psum(dprob_part, "et")
    dprob_mine = lax.dynamic_slice_in_dim(dprob_all, first_row, own_rows, 0)
    route_mine = lax.dynamic_slice_in_dim(route_b, first_row, own_rows, 0)
    sigma_mine = lax.dynamic_slice_in_dim(sigma_b, first_row, own_rows, 0)
    onehot_mine = lax.dynamic_slice_in_dim(onehot_b, first_row, own_rows, 0)
    slope = route_mine * dprob_mine * sigma_mine * (1.0 - sigma_mine)
    router_wide = w_router.astype(jnp.float32)
    spread = router_wide[:, 0][None, :] - jnp.dot(
        onehot_mine, router_wide.T, precision=lax.Precision.HIGHEST
    )
    dnormed = slope[:, None] * spread
    scaled_rows = dnormed * gain.astype(jnp.float32)
    normalized_input = backward_wide_rows * backward_inverse_norm
    norm_input_gradient = backward_inverse_norm * (
        scaled_rows
        - normalized_input * jnp.mean(scaled_rows * normalized_input, axis=-1, keepdims=True)
    )
    input_grad = (grad_out.astype(jnp.float32) + norm_input_gradient).astype(jnp.bfloat16)
    fwd_in = from_behind(layer_out, "section", 1)
    incoming_gradient = from_behind(input_grad, "section", -1)
    return (fwd_in[None], incoming_gradient[None], dact[None])


def solution(mesh):
    placed = (
        P("section", "et", None),
        P("section", None, "et"),
        P("section", None, None),
        P("section", "et", None),
        P("section", None, "et"),
        P("section", None, None),
        P("section", "et", None),
        P("section", None),
        P("section", None, None),
        P("section", "et", None),
    )
    return jax.shard_map(
        shards,
        mesh=mesh,
        in_specs=placed,
        out_specs=(P("section", "et", None), P("section", "et", None), P("section", None, "et")),
        check_vma=False,
    )
```

profile of v0, /device:TPU:6, one launch (start us, length us, event | category | flops | bytes accessed | tf_op | source)
XLA Modules:
  0.0 256.7 jit_solution(1746351903962819599)
XLA Ops:
  7.2 0.9 convert_reduce_fusion.5
  8.1 1.4 convert_reduce_fusion
  9.5 0.3 reduce-window.34
  10.6 0.7 compare_select_fusion.8
  11.3 0.7 compare_select_fusion.2
  11.9 1.4 scatter_custom_fusion
  13.4 0.7 mul.173
  14.1 1.0 fusion.22
  15.1 1.1 fusion.6
  16.3 17.6 %all-gather.1 = bf16[16,16,8]{1,2,0:T(8,128)(2,1)S(1)} all-gather(bf16[1,16,8]{1,2,0:T(8,128)(2,1)S(1)} %fusion.6), channel_id=1, replica_groups=mesh['section'=32,'et'=16] {'et'}, dimensions={0}, use_global_device_ids=true | all-gather | bytes 4352 | tf_op jit(solution)/shard_map/all_gather | solution.py:69
  34.1 1.9 gather_fusion
  36.0 1.3 gather_fusion.1
  37.3 1.5 fusion
  38.8 0.7 all-gather.5.cloned.1.call-update
  39.6 0.6 pad_clamp_fusion.2
  40.4 1.0 fusion.7
  41.4 0.3 reduce-window.50
  42.0 0.3 reduce-window.48
  42.6 1.2 compare_select_fusion
  43.8 1.4 scatter_custom_fusion.1
  45.3 0.7 dynamic-slice_compare_fusion
  45.9 15.0 %all-gather.2 = bf16[16,16,8]{1,2,0:T(8,128)(2,1)S(1)} all-gather(bf16[1,16,8]{1,2,0:T(8,128)(2,1)S(1)} %fusion.7), channel_id=1, replica_groups=mesh['section'=32,'et'=16] {'et'}, dimensions={0}, use_global_device_ids=true | all-gather | bytes 4352 | tf_op jit(solution)/shard_map/all_gather | solution.py:70
  61.0 0.6 pad_clamp_fusion.1
  61.7 0.6 broadcast_compare_fusion.2
  62.2 0.6 iota_compare_fusion
  62.8 0.6 divide_multiply_fusion
  63.4 0.6 add_divide_fusion
  63.9 1.4 slice_convert_fusion
  65.3 92.2 %all-reduce.2.cloned.1.call-done = bf16[128,3072]{1,0:T(8,128)(2,1)} async-done(((bf16[128,3072]{1,0:T(8,128)(2,1)}), bf16[128,3072]{1,0:T(8,128)(2,1)}) %all-reduce.2.cloned.1.call-update) | async-done | bytes 786448 | tf_op jit(solution)/shard_map/psum | solution.py:80
  157.6 2.4 convert_element_type.106
  160.0 2.2 gather_fusion.2
  162.2 0.8 fusion.23
  163.0 3.5 %collective-permute-start = (bf16[16,3072]{1,0:T(8,128)(2,1)S(1)}, bf16[16,3072]{1,0:T(8,128)(2,1)}, u32[]{:S(2)}, u32[]{:S(2)}) collective-permute-start(bf16[16,3072]{1,0:T(8,128)(2,1)S(1)} %fusion.23), channel_id=1, source_target_pairs={{0,16},{16,32},{32,48},{48,64},{64,80},{80,96},{96,112},{112,128},... | collective-permute-start | bytes 294920 | tf_op jit(solution)/shard_map/ppermute | solution.py:10
  166.5 0.6 pad_clamp_fusion
  167.2 2.4 collective-permute-done
  169.6 32.3 %all-gather.5.cloned.1.call-done = bf16[1,256,3072]{2,1,0:T(8,128)(2,1)} async-done(((bf16[1,16,3072]{2,1,0:T(8,128)(2,1)}), bf16[1,256,3072]{2,1,0:T(8,128)(2,1)}) %all-gather.5.cloned.1.call-update) | async-done | bytes 1572880 | tf_op jit(solution)/shard_map/all_gather | solution.py:71
  201.9 4.5 %gather_fusion.3 = bf16[128,3072]{1,0:T(8,128)(2,1)} fusion(bf16[256,3072]{1,0:T(8,128)(2,1)} %bitcast.108, s32[1024]{0:T(1024)} %pad_clamp_fusion.1), kind=kCustom, calls=%fused_computation.3 | custom fusion | bytes 1573376 | tf_op jit(solution)/shard_map/gather | solution.py:89
  206.3 2.3 fusion.3
  208.7 1.8 gather_fusion.4
  210.5 1.3 fusion.8
  211.8 24.9 %psum.15 = f32[256]{0:T(256)S(1)} all-reduce(f32[256]{0:T(256)S(1)} %fusion.8), channel_id=1, replica_groups=mesh['section'=32,'et'=16] {'et'}, use_global_device_ids=true, to_apply=%region_22.23 | all-reduce | flops 256 | bytes 2048 | tf_op jit(solution)/shard_map/psum | solution.py:94
  236.8 1.2 fusion.17
  238.0 1.0 fusion.21
  239.0 2.8 %collective-permute-start.1 = (bf16[16,3072]{1,0:T(8,128)(2,1)S(1)}, bf16[16,3072]{1,0:T(8,128)(2,1)S(1)}, u32[]{:S(2)}, u32[]{:S(2)}) collective-permute-start(bf16[16,3072]{1,0:T(8,128)(2,1)S(1)} %fusion.21), channel_id=1, source_target_pairs={{16,0},{32,16},{48,32},{64,48},{80,64},{96,80},{112,96},{128,112},... | collective-permute-start | bytes 294920 | tf_op jit(solution)/shard_map/ppermute | solution.py:10
  241.8 1.9 fusion.10
  243.7 4.0 %collective-permute-done.1 = bf16[16,3072]{1,0:T(8,128)(2,1)S(1)} collective-permute-done((bf16[16,3072]{1,0:T(8,128)(2,1)S(1)}, bf16[16,3072]{1,0:T(8,128)(2,1)S(1)}, u32[]{:S(2)}, u32[]{:S(2)}) %collective-permute-start.1) | collective-permute-done | bytes 98336 | tf_op jit(solution)/shard_map/ppermute | solution.py:10
  247.6 1.5 copy.20
  249.2 0.6 copy.21
  (63 shorter events, 2.1 us)
Async XLA Ops:
  7.2 30.1 %copy-start = (bf16[1,512,3072]{2,1,0:T(8,128)(2,1)S(1)}, bf16[1,512,3072]{2,1,0:T(8,128)(2,1)}, u32[]{:S(2)}) copy-start(bf16[1,512,3072]{2,1,0:T(8,128)(2,1)} %param.19) | copy-start | bytes 9437188
  7.2 150.4 %all-reduce.2.cloned.1.call-start = ((), (), s32[]{:S(2)}) async-start(), calls=%async_computation | async-start | bytes 1572864 | tf_op jit(solution)/shard_map/psum | solution.py:80
  34.0 6.2 %copy-start.2 = (bf16[1,16,3072]{2,1,0:T(8,128)(2,1)S(1)}, bf16[1,16,3072]{2,1,0:T(8,128)(2,1)}, u32[]{:S(2)}) copy-start(bf16[1,16,3072]{2,1,0:T(8,128)(2,1)} %param.13) | copy-start | bytes 294916
  35.9 25.7 %copy-start.4 = (s32[1,256,2]{1,2,0:T(2,128)S(1)}, s32[1,256,2]{1,2,0:T(2,128)}, u32[]{:S(2)}) copy-start(s32[1,256,2]{1,2,0:T(2,128)} %param.15) | copy-start | bytes 6148
  38.8 123.5 %copy-start.1 = (bf16[1,16,3072]{2,1,0:T(8,128)(2,1)S(1)}, bf16[1,16,3072]{2,1,0:T(8,128)(2,1)}, u32[]{:S(2)}) copy-start(bf16[1,16,3072]{2,1,0:T(8,128)(2,1)} %param.10) | copy-start | bytes 294916
  38.8 163.1 %all-gather.5.cloned.1.call-start = ((), (), s32[]{:S(2)}) async-start(), calls=%async_computation.1 | async-start | bytes 1671168 | tf_op jit(solution)/shard_map/all_gather | solution.py:71
  40.4 1.0 copy-start.9
  163.0 6.6 %collective-permute-start = (bf16[16,3072]{1,0:T(8,128)(2,1)S(1)}, bf16[16,3072]{1,0:T(8,128)(2,1)}, u32[]{:S(2)}, u32[]{:S(2)}) collective-permute-start(bf16[16,3072]{1,0:T(8,128)(2,1)S(1)} %fusion.23), channel_id=1, source_target_pairs={{0,16},{16,32},{32,48},{48,64},{64,80},{80,96},{96,112},{112,128},... | collective-permute-start | bytes 294920 | tf_op jit(solution)/shard_map/ppermute | solution.py:10
  208.7 1.8 copy-start.8
  208.7 28.0 %copy-start.6 = (f32[256]{0:T(256)S(1)}, f32[256]{0:T(256)}, u32[]{:S(2)}) copy-start(f32[256]{0:T(256)} %add_divide_fusion) | copy-start | bytes 3076
  208.7 28.1 %copy-start.3 = (f32[3072,1]{0,1:T(1,128)S(1)}, f32[3072,1]{0,1:T(1,128)}, u32[]{:S(2)}) copy-start(f32[3072,1]{0,1:T(1,128)} %slice_convert_fusion) | copy-start | bytes 36868
  208.7 28.1 %copy-start.7 = (pred[256,8]{0,1:T(8,128)(4,1)S(1)}, pred[256,8]{0,1:T(8,128)(4,1)}, u32[]{:S(2)}) copy-start(pred[256,8]{0,1:T(8,128)(4,1)} %iota_compare_fusion) | copy-start | bytes 6148
  208.7 33.1 %copy-start.5 = (f32[256,1]{0,1:T(1,128)S(1)}, f32[256,1]{0,1:T(1,128)}, u32[]{:S(2)}) copy-start(f32[256,1]{0,1:T(1,128)} %get-tuple-element.14) | copy-start | bytes 3076
  239.0 8.6 %collective-permute-start.1 = (bf16[16,3072]{1,0:T(8,128)(2,1)S(1)}, bf16[16,3072]{1,0:T(8,128)(2,1)S(1)}, u32[]{:S(2)}, u32[]{:S(2)}) collective-permute-start(bf16[16,3072]{1,0:T(8,128)(2,1)S(1)} %fusion.21), channel_id=1, source_target_pairs={{16,0},{32,16},{48,32},{64,48},{80,64},{96,80},{112,96},{128,112},... | collective-permute-start | bytes 294920 | tf_op jit(solution)/shard_map/ppermute | solution.py:10
Sparse Core Ops, SparseCore 0:
  38.9 118.5 all-reduce.1
  159.7 42.1 all-gather.4
where the time goes:
time: 257 us
  waiting for transfers between devices  132 us (51%)
  blocking collectives  57.5 us (22%)
  other arithmetic  22.1 us (9%)
  local copies, waits for them, and re-layouts  17.6 us (7%)
  between operations  14.3 us (6%)
  matrix products  7.15 us (3%)
  starting transfers between devices  6.38 us (2%)
    psum x1, waiting for transfers between devices, shards(): summed = lax.psum(compact.astype(jnp.bfloat16), 'et').astype(jnp.float32)  92.2 us
    all_gather x1, waiting for transfers between devices, shards(): lax.all_gather(grad_out, 'et', axis=0, tiled=True)  32.3 us
    psum x1, blocking collectives, shards(): dprob_all = lax.psum(dprob_part, 'et')  24.9 us
    all_gather x1, blocking collectives, shards(): lax.all_gather(logit_f, 'et', axis=0, tiled=True)  17.6 us
    all_gather x1, blocking collectives, shards(): lax.all_gather(logit_b, 'et', axis=0, tiled=True)  15 us
    ppermute x2, waiting for transfers between devices, from_behind(): lax.ppermute(value, axis, [(source, source + steps) for source in range(f...  6.38 us
    ppermute x2, starting transfers between devices, from_behind(): lax.ppermute(value, axis, [(source, source + steps) for source in range(f...  6.3 us
  transfers between devices with their start and end apart: 4, of which 4 were waited for; matrix products, arithmetic and copies ran while one was open for 7% of the time, Pallas kernels for 0%

commit v1 on v0

--- a/solution.py
+++ b/solution.py
@@ -91,7 +91,11 @@
     back_up = spread_back(up_compact, member_b, place_b, capacity)
     dact = (backward_coefficient[:, None] * back_up).astype(jnp.bfloat16)
     dprob_part = jnp.sum(act_bwd.astype(jnp.float32) * back_up, axis=1)
-    dprob_all = lax.psum(dprob_part, "et")
+    dprob_all = dprob_part
+    for hop in (1, 2, 4, 8):
+        dprob_all = dprob_all + lax.ppermute(
+            dprob_all, "et", [(dev, dev ^ hop) for dev in range(16)]
+        )
     dprob_mine = lax.dynamic_slice_in_dim(dprob_all, first_row, own_rows, 0)
     route_mine = lax.dynamic_slice_in_dim(route_b, first_row, own_rows, 0)
     sigma_mine = lax.dynamic_slice_in_dim(sigma_b, first_row, own_rows, 0)

time: 257 us -> 218 us (0.85)
  waiting for transfers between devices: 132 us -> 103 us
  blocking collectives: 57.5 us -> 32.7 us
  starting transfers between devices: 6.38 us -> 20.2 us
    all_gather x1, waiting for transfers between devices: 32.3 us -> 0.01 us  [shards(): lax.all_gather(grad_out, 'et', axis=0, tiled=True)]
    psum x1 -> x0, blocking collectives: 24.9 us -> none  [shards(): dprob_all = lax.psum(dprob_part, 'et')]
    ppermute x0 -> x4, starting transfers between devices: none -> 14.3 us  [shards(): lax.ppermute(dprob_all, 'et', [(dev, dev ^ hop) for dev in range(16)])]
    psum x1, waiting for transfers between devices: 92.2 us -> 95.1 us  [shards(): summed = lax.psum(compact.astype(jnp.bfloat16), 'et').astype(jnp.float32)]
  transfers between devices with their start and end apart: 4 -> 8, of which waited for: 4 -> 3; matrix products, arithmetic and copies ran while one was open for 7% -> 19% of each run, Pallas kernels for 0% -> 0%
where the time goes in v1:
time: 218 us; the launch traced here: 216 us
  waiting for transfers between devices  103 us (47%)
  blocking collectives  32.7 us (15%)
  other arithmetic  22.8 us (10%)
  starting transfers between devices  20.2 us (9%)
  local copies, waits for them, and re-layouts  16.6 us (8%)
  between operations  14.4 us (7%)
  matrix products  6.5 us (3%)
    psum x1, waiting for transfers between devices, shards(): summed = lax.psum(compact.astype(jnp.bfloat16), 'et').astype(jnp.float32)  95.1 us
    all_gather x1, blocking collectives, shards(): lax.all_gather(logit_f, 'et', axis=0, tiled=True)  17.6 us
    all_gather x1, blocking collectives, shards(): lax.all_gather(logit_b, 'et', axis=0, tiled=True)  15 us
    ppermute x4, starting transfers between devices, shards(): lax.ppermute(dprob_all, 'et', [(dev, dev ^ hop) for dev in range(16)])  14.3 us
    ppermute x2, starting transfers between devices, from_behind(): lax.ppermute(value, axis, [(source, source + steps) for source in range(f...  5.84 us
    ppermute x2, waiting for transfers between devices, from_behind(): lax.ppermute(value, axis, [(source, source + steps) for source in range(f...  4.42 us
  transfers between devices with their start and end apart: 8, of which 3 were waited for; matrix products, arithmetic and copies ran while one was open for 19% of the time, Pallas kernels for 0%

profile of v1, /device:TPU:6, one launch (start us, length us, event | category | flops | bytes accessed | tf_op | source)
XLA Modules:
  0.0 215.7 jit_solution(10610477418814259614)
XLA Ops:
  7.2 0.7 all-gather.5.cloned.1.call-update
  8.0 1.5 convert_reduce_fusion
  10.3 0.7 mul.173
  11.0 1.0 fusion.22
  12.1 1.1 fusion.6
  13.2 17.6 %all-gather.1 = bf16[16,16,8]{1,2,0:T(8,128)(2,1)S(1)} all-gather(bf16[1,16,8]{1,2,0:T(8,128)(2,1)S(1)} %fusion.6), channel_id=1, replica_groups=mesh['section'=32,'et'=16] {'et'}, dimensions={0}, use_global_device_ids=true | all-gather | bytes 4352 | tf_op jit(solution)/shard_map/all_gather | solution.py:69
  31.2 0.7 compare_select_fusion.8
  31.9 0.7 compare_select_fusion.2
  32.6 1.4 scatter_custom_fusion
  34.0 1.9 gather_fusion
  35.9 0.7 convert_reduce_fusion.5
  36.7 1.3 gather_fusion.1
  38.0 1.5 fusion
  39.5 0.5 broadcast_compare_fusion.2
  40.2 0.6 iota_compare_fusion
  40.8 0.6 slice_convert_fusion
  41.6 15.0 %all-gather.2 = bf16[16,16,8]{1,2,0:T(8,128)(2,1)S(1)} all-gather(bf16[1,16,8]{1,2,0:T(8,128)(2,1)S(1)} %fusion.7), channel_id=1, replica_groups=mesh['section'=32,'et'=16] {'et'}, dimensions={0}, use_global_device_ids=true | all-gather | bytes 4352 | tf_op jit(solution)/shard_map/all_gather | solution.py:70
  58.0 0.7 compare_select_fusion
  58.7 1.4 scatter_custom_fusion.1
  60.1 0.7 compare_select_fusion.6
  60.8 0.6 divide_multiply_fusion
  61.4 4.3 %gather_fusion.3 = bf16[128,3072]{1,0:T(8,128)(2,1)} fusion(bf16[256,3072]{1,0:T(8,128)(2,1)} %bitcast.108, s32[1024]{0:T(1024)S(1)} %pad_clamp_fusion.1), kind=kCustom, calls=%fused_computation.3 | custom fusion | bytes 1573376 | tf_op jit(solution)/shard_map/gather | solution.py:89
  65.7 2.3 %fusion.3 = f32[128,512]{1,0:T(8,128)S(1)} fusion(bf16[128,3072]{1,0:T(8,128)(2,1)} %gather_fusion.3, bf16[1,512,3072]{2,1,0:T(8,128)(2,1)S(1)} %copy-done), kind=kOutput, calls=%fused_computation.12 | convolution fusion | flops 402653184 | bytes 4194304 | tf_op jit(solution)/shard_map/dot_general | solution.py:88
  68.0 1.8 gather_fusion.4
  69.8 1.4 fusion.8
  71.1 2.3 %collective-permute-start.1 = (f32[256]{0:T(256)S(1)}, f32[256]{0:T(256)S(1)}, u32[]{:S(2)}, u32[]{:S(2)}) collective-permute-start(f32[256]{0:T(256)S(1)} %fusion.8), channel_id=1, source_target_pairs={{0,1},{1,0},{2,3},{3,2},{4,5},{5,4},{6,7},{7,6},{8,9},{9,8},{10,11... | collective-permute-start | bytes 3080 | tf_op jit(solution)/shard_map/ppermute | solution.py:96
  73.4 1.3 pad_clamp_fusion.2
  74.7 0.6 add.148
  75.3 3.1 %collective-permute-start.2 = (f32[256]{0:T(256)}, f32[256]{0:T(256)}, u32[]{:S(2)}, u32[]{:S(2)}) collective-permute-start(f32[256]{0:T(256)} %add.148), channel_id=1, source_target_pairs={{0,2},{1,3},{2,0},{3,1},{4,6},{5,7},{6,4},{7,5},{8,10},{9,11},{10,... | collective-permute-start | bytes 3080 | tf_op jit(solution)/shard_map/ppermute | solution.py:96
  78.4 0.7 dynamic-slice_compare_fusion
  79.0 95.1 %all-reduce.2.cloned.1.call-done = bf16[128,3072]{1,0:T(8,128)(2,1)} async-done(((bf16[128,3072]{1,0:T(8,128)(2,1)}), bf16[128,3072]{1,0:T(8,128)(2,1)}) %all-reduce.2.cloned.1.call-update) | async-done | bytes 786448 | tf_op jit(solution)/shard_map/psum | solution.py:80
  174.2 2.4 %convert_element_type.106 = f32[128,3072]{1,0:T(8,128)} convert(bf16[128,3072]{1,0:T(8,128)(2,1)} %all-reduce.2.cloned.1.call-done) | non-fusion elementwise | flops 393216 | bytes 2359296 | tf_op jit(solution)/shard_map/convert_element_type | solution.py:80
  176.6 2.2 %gather_fusion.2 = f32[16,3072]{1,0:T(8,128)S(1)} fusion(f32[128,3072]{1,0:T(8,128)} %convert_element_type.106, s32[1024]{0:T(1024)} %pad_clamp_fusion.2), kind=kCustom, calls=%fused_computation.2 | custom fusion | bytes 393280 | tf_op jit(solution)/shard_map/gather | solution.py:43
  178.8 0.7 add.149
  179.5 2.6 %collective-permute-start.3 = (f32[256]{0:T(256)S(1)}, f32[256]{0:T(256)S(1)}, u32[]{:S(2)}, u32[]{:S(2)}) collective-permute-start(f32[256]{0:T(256)S(1)} %add.149), channel_id=1, source_target_pairs={{0,4},{1,5},{2,6},{3,7},{4,0},{5,1},{6,2},{7,3},{8,12},{9,13},{10,... | collective-permute-start | bytes 3080 | tf_op jit(solution)/shard_map/ppermute | solution.py:96
  182.1 0.8 fusion.23
  182.9 3.5 %collective-permute-start = (bf16[16,3072]{1,0:T(8,128)(2,1)S(1)}, bf16[16,3072]{1,0:T(8,128)(2,1)S(1)}, u32[]{:S(2)}, u32[]{:S(2)}) collective-permute-start(bf16[16,3072]{1,0:T(8,128)(2,1)S(1)} %fusion.23), channel_id=1, source_target_pairs={{0,16},{16,32},{32,48},{48,64},{64,80},{80,96},{96,112},{112,128},... | collective-permute-start | bytes 294920 | tf_op jit(solution)/shard_map/ppermute | solution.py:10
  186.5 6.4 %collective-permute-start.4 = (f32[256]{0:T(256)S(1)}, f32[256]{0:T(256)S(1)}, u32[]{:S(2)}, u32[]{:S(2)}) collective-permute-start(f32[256]{0:T(256)S(1)} %add.150), channel_id=1, source_target_pairs={{0,8},{1,9},{2,10},{3,11},{4,12},{5,13},{6,14},{7,15},{8,0},{9,1},... | collective-permute-start | bytes 3080 | tf_op jit(solution)/shard_map/ppermute | solution.py:96
  192.8 0.7 add_divide_fusion
  193.5 2.3 %collective-permute-done.4 = f32[256]{0:T(256)S(1)} collective-permute-done((f32[256]{0:T(256)S(1)}, f32[256]{0:T(256)S(1)}, u32[]{:S(2)}, u32[]{:S(2)}) %collective-permute-start.4) | collective-permute-done | bytes 1056 | tf_op jit(solution)/shard_map/ppermute | solution.py:96
  195.8 0.7 subtract_multiply_fusion
  196.6 1.4 fusion.17
  197.9 1.0 fusion.21
  199.0 2.3 %collective-permute-start.5 = (bf16[16,3072]{1,0:T(8,128)(2,1)S(1)}, bf16[16,3072]{1,0:T(8,128)(2,1)S(1)}, u32[]{:S(2)}, u32[]{:S(2)}) collective-permute-start(bf16[16,3072]{1,0:T(8,128)(2,1)S(1)} %fusion.21), channel_id=1, source_target_pairs={{16,0},{32,16},{48,32},{64,48},{80,64},{96,80},{112,96},{128,112},... | collective-permute-start | bytes 294920 | tf_op jit(solution)/shard_map/ppermute | solution.py:10
  201.3 1.9 fusion.10
  203.2 4.4 %collective-permute-done.5 = bf16[16,3072]{1,0:T(8,128)(2,1)S(1)} collective-permute-done((bf16[16,3072]{1,0:T(8,128)(2,1)S(1)}, bf16[16,3072]{1,0:T(8,128)(2,1)S(1)}, u32[]{:S(2)}, u32[]{:S(2)}) %collective-permute-start.5) | collective-permute-done | bytes 98336 | tf_op jit(solution)/shard_map/ppermute | solution.py:10
  207.6 0.6 copy.20
  208.2 0.6 copy.21
  (72 shorter events, 3.1 us)
Async XLA Ops:
  7.2 30.8 %copy-start = (bf16[1,512,3072]{2,1,0:T(8,128)(2,1)S(1)}, bf16[1,512,3072]{2,1,0:T(8,128)(2,1)}, u32[]{:S(2)}) copy-start(bf16[1,512,3072]{2,1,0:T(8,128)(2,1)} %param.19) | copy-start | bytes 9437188
  7.2 54.2 %all-gather.5.cloned.1.call-start = ((), (), s32[]{:S(2)}) async-start(), calls=%async_computation.1 | async-start | bytes 1671168 | tf_op jit(solution)/shard_map/all_gather | solution.py:71
  7.9 166.2 %all-reduce.2.cloned.1.call-start = ((), (), s32[]{:S(2)}) async-start(), calls=%async_computation | async-start | bytes 1572864 | tf_op jit(solution)/shard_map/psum | solution.py:80
  34.0 5.5 %copy-start.5 = (s32[1,256,2]{1,2,0:T(2,128)S(1)}, s32[1,256,2]{1,2,0:T(2,128)}, u32[]{:S(2)}) copy-start(s32[1,256,2]{1,2,0:T(2,128)} %param.15) | copy-start | bytes 6148
  34.0 6.1 %copy-start.3 = (bf16[1,16,3072]{2,1,0:T(8,128)(2,1)S(1)}, bf16[1,16,3072]{2,1,0:T(8,128)(2,1)}, u32[]{:S(2)}) copy-start(bf16[1,16,3072]{2,1,0:T(8,128)(2,1)} %param.13) | copy-start | bytes 294916
  34.0 6.8 %copy-start.7 = (bf16[1,3072,8]{1,2,0:T(8,128)(2,1)S(1)}, bf16[1,3072,8]{1,2,0:T(8,128)(2,1)}, u32[]{:S(2)}) copy-start(bf16[1,3072,8]{1,2,0:T(8,128)(2,1)} %param.18) | copy-start | bytes 147460
  39.5 21.8 %copy-start.6 = (f32[256]{0:T(256)}, f32[256]{0:T(256)S(1)}, u32[]{:S(2)}) copy-start(f32[256]{0:T(256)S(1)} %convert_reduce_fusion.4) | copy-start | bytes 3076
  40.2 21.1 %copy-start.8 = (f32[16]{0:T(128)}, f32[16]{0:T(128)S(1)}, u32[]{:S(2)}) copy-start(f32[16]{0:T(128)S(1)} %add_rsqrt_fusion) | copy-start | bytes 196
  56.8 4.6 %copy-start.4 = (f32[256]{0:T(256)}, f32[256]{0:T(256)S(1)}, u32[]{:S(2)}) copy-start(f32[256]{0:T(256)S(1)} %select_reduce_fusion) | copy-start | bytes 3076
  69.8 112.4 %copy-start.1 = (bf16[1,16,3072]{2,1,0:T(8,128)(2,1)S(1)}, bf16[1,16,3072]{2,1,0:T(8,128)(2,1)}, u32[]{:S(2)}) copy-start(bf16[1,16,3072]{2,1,0:T(8,128)(2,1)} %param.10) | copy-start | bytes 294916
  69.8 128.2 %copy-start.2 = (bf16[1,16,3072]{2,1,0:T(8,128)(2,1)S(1)}, bf16[1,16,3072]{2,1,0:T(8,128)(2,1)}, u32[]{:S(2)}) copy-start(bf16[1,16,3072]{2,1,0:T(8,128)(2,1)} %param.16) | copy-start | bytes 294916
  71.1 3.5 %collective-permute-start.1 = (f32[256]{0:T(256)S(1)}, f32[256]{0:T(256)S(1)}, u32[]{:S(2)}, u32[]{:S(2)}) collective-permute-start(f32[256]{0:T(256)S(1)} %fusion.8), channel_id=1, source_target_pairs={{0,1},{1,0},{2,3},{3,2},{4,5},{5,4},{6,7},{7,6},{8,9},{9,8},{10,11... | collective-permute-start | bytes 3080 | tf_op jit(solution)/shard_map/ppermute | solution.py:96
  75.3 103.6 %collective-permute-start.2 = (f32[256]{0:T(256)}, f32[256]{0:T(256)}, u32[]{:S(2)}, u32[]{:S(2)}) collective-permute-start(f32[256]{0:T(256)} %add.148), channel_id=1, source_target_pairs={{0,2},{1,3},{2,0},{3,1},{4,6},{5,7},{6,4},{7,5},{8,10},{9,11},{10,... | collective-permute-start | bytes 3080 | tf_op jit(solution)/shard_map/ppermute | solution.py:96
  179.5 6.9 %collective-permute-start.3 = (f32[256]{0:T(256)S(1)}, f32[256]{0:T(256)S(1)}, u32[]{:S(2)}, u32[]{:S(2)}) collective-permute-start(f32[256]{0:T(256)S(1)} %add.149), channel_id=1, source_target_pairs={{0,4},{1,5},{2,6},{3,7},{4,0},{5,1},{6,2},{7,3},{8,12},{9,13},{10,... | collective-permute-start | bytes 3080 | tf_op jit(solution)/shard_map/ppermute | solution.py:96
  182.9 10.6 %collective-permute-start = (bf16[16,3072]{1,0:T(8,128)(2,1)S(1)}, bf16[16,3072]{1,0:T(8,128)(2,1)S(1)}, u32[]{:S(2)}, u32[]{:S(2)}) collective-permute-start(bf16[16,3072]{1,0:T(8,128)(2,1)S(1)} %fusion.23), channel_id=1, source_target_pairs={{0,16},{16,32},{32,48},{48,64},{64,80},{80,96},{96,112},{112,128},... | collective-permute-start | bytes 294920 | tf_op jit(solution)/shard_map/ppermute | solution.py:10
  186.5 9.4 %collective-permute-start.4 = (f32[256]{0:T(256)S(1)}, f32[256]{0:T(256)S(1)}, u32[]{:S(2)}, u32[]{:S(2)}) collective-permute-start(f32[256]{0:T(256)S(1)} %add.150), channel_id=1, source_target_pairs={{0,8},{1,9},{2,10},{3,11},{4,12},{5,13},{6,14},{7,15},{8,0},{9,1},... | collective-permute-start | bytes 3080 | tf_op jit(solution)/shard_map/ppermute | solution.py:96
  199.0 8.6 %collective-permute-start.5 = (bf16[16,3072]{1,0:T(8,128)(2,1)S(1)}, bf16[16,3072]{1,0:T(8,128)(2,1)S(1)}, u32[]{:S(2)}, u32[]{:S(2)}) collective-permute-start(bf16[16,3072]{1,0:T(8,128)(2,1)S(1)} %fusion.21), channel_id=1, source_target_pairs={{16,0},{32,16},{48,32},{64,48},{80,64},{96,80},{112,96},{128,112},... | collective-permute-start | bytes 294920 | tf_op jit(solution)/shard_map/ppermute | solution.py:10
Sparse Core Ops, SparseCore 0:
  10.1 45.9 all-gather.4
  58.4 115.7 all-reduce.1
